TPU v7x, 256 devices: a whole 4x4x8 slice. The times are simulated.
256 devices in a mesh: circ: 8 (over y_lo, x), span: 32 (over y_hi, z, core).
Axes of the slice: x: 4, y: 4 (y_hi: 2, y_lo: 2; y = y_hi * 2 + y_lo), z: 8, core: 2. Of those that a mesh axis runs over, the one named last changes fastest.
Arguments:
- q_old: float32 [5, 32, 4096, 128], P(None, 'circ', 'span'), may hold values from -6 to 6
- pseudo_rate: float32 [32, 4096, 128], P('circ', 'span'), may hold values from 0.15 to 0.45
- flux_jacobians: float32 [3, 5, 5], replicated, may hold values from -2.5 to 2.5
- rotor_face: float32 [5, 32, 4096], P(None, 'circ', 'span'), may hold values from -6 to 6
- offsets: int32 [4096], P('span'), may hold values from 0 to 31
- owners: int32 [8, 128, 4], P('circ', 'span'), may hold values from 0 to 31, all different within a row; in each aligned block of 4 rows (0 to 3, 4 to 7, ..., all dimensions but the last counted through in order) at most 2 rows name the same one
- slots: int32 [8, 128, 4], P('circ', 'span'), may hold values from 0 to 3
- weight_idx: int32 [8, 128, 4], P('circ', 'span'), may hold values from 0 to 15
- weight_table: float32 [16], replicated, may hold values from 0.3 to 1
Outputs:
- q_new: float32 [5, 32, 4096, 128], P(None, 'circ', 'span')
Inputs may be any that keep to these rules, and one draw needn't show every extreme that they name: The 4 owners of one rotor panel differ; among the 4 rotor panels of one device in one circumferential block, no owner is named more than 2 times, and that count is reached.
All inputs are finite; a program needn't handle non-finite values.
Results may differ from a plain program's by a relative error of at most 0.000068.
Values sent between devices are 32-bit elements; how exact they have to be, the bound alone decides.
No kernel may reach another device: no remote copies, remote signals or barrier semaphores. Data moves between devices by JAX's collectives and lax.ppermute only.
A program may use at most 64 MiB of HBM per device.

v0:
```python
import jax
import jax.numpy as jnp
from jax import lax
from jax.sharding import PartitionSpec as P

NF = 5
KP_DEV = 4
PW = 32


inv_step = 0.5
viscosity = 0.1


def with_halo(block, sides, width):
    for axis, dim in sides:
        count = lax.axis_size(axis)
        forward = [(i, i + 1) for i in range(count - 1)]
        forward.append((count - 1, 0))
        backward = [(target, source) for source, target in forward]
        low = lax.ppermute(
            lax.slice_in_dim(block, block.shape[dim] - width, None, axis=dim), axis, forward
        )
        high = lax.ppermute(lax.slice_in_dim(block, 0, width, axis=dim), axis, backward)
        block = jnp.concatenate([low, block, high], axis=dim)
    return block


def contract(matrix, values):
    return jnp.einsum("fg,gtsa->ftsa", matrix, values, precision=lax.Precision.HIGHEST)


def advance(padded, current, previous, rate_cells, inlet_plane, jacobians):
    circ_up = padded[:, 2:, 1:-1]
    circ_down = padded[:, :-2, 1:-1]
    span_up = padded[:, 1:-1, 2:]
    span_down = padded[:, 1:-1, :-2]
    zero_column = jnp.zeros_like(current[..., :1])
    axial_up = jnp.concatenate([current[..., 1:], zero_column], axis=-1)
    axial_down = jnp.concatenate([inlet_plane[..., None], current[..., :-1]], axis=-1)
    convection = contract(jacobians[0], circ_up - circ_down)
    convection = convection + contract(jacobians[1], span_up - span_down)
    convection = convection + contract(jacobians[2], axial_up - axial_down)
    laplacian = (
        circ_up + circ_down + (span_up + span_down) + (axial_up + axial_down) - 6.0 * current
    )
    residual = inv_step * (current - previous) + 0.5 * convection - viscosity * laplacian
    return current - rate_cells[None] * residual


def wall_zero(field_array, width):
    span_index = lax.axis_index("span")
    span_count = lax.axis_size("span")
    length = field_array.shape[2]
    position = jnp.arange(length, dtype=jnp.int32)
    at_hub = jnp.logical_and(span_index == 0, position < width)
    at_tip = jnp.logical_and(span_index == span_count - 1, position >= length - width)
    keeping = jnp.logical_not(jnp.logical_or(at_hub, at_tip)).astype(field_array.dtype)
    keeping = keeping.reshape(1, 1, length, 1)
    return field_array * keeping


def body(
    q_old, pseudo_rate, flux_jacobians, rotor_face, offsets, owners, slots, weight_idx, weight_table
):
    circ_count = lax.axis_size("circ")
    rows_local = rotor_face.shape[1]
    total_rows = rows_local * circ_count
    row_iota = jnp.arange(rows_local, dtype=jnp.int32)
    all_rows = lax.all_gather(rotor_face, "circ", axis=1, tiled=True)
    first_row = lax.axis_index("circ") * rows_local
    source_rows = (first_row + row_iota[:, None] - offsets[None, :]) % total_rows
    rotated = jnp.take_along_axis(all_rows, source_rows[None], axis=1)
    panels = rotated.reshape(NF, rows_local, KP_DEV, PW)
    table_ids = jnp.arange(weight_table.shape[0], dtype=jnp.int32)
    weights = jnp.sum(jnp.where(weight_idx[..., None] == table_ids, weight_table, 0.0), axis=-1)
    targets = owners[0] * KP_DEV + slots[0]
    local_weights = weights[0]
    panel_ids = jnp.arange(KP_DEV * lax.axis_size("span"), dtype=jnp.int32)
    mixing = jnp.sum(
        jnp.where(targets[None] == panel_ids[:, None, None], local_weights[None], 0.0), axis=-1
    )
    own_panels = lax.psum_scatter(
        jnp.einsum("gk,ftkp->gftp", mixing, panels, precision=lax.Precision.HIGHEST),
        "span",
        scatter_dimension=0,
        tiled=True,
    )
    inlet_plane = jnp.transpose(own_panels, (1, 2, 0, 3)).reshape(NF, rows_local, KP_DEV * PW)

    def sweep(current):
        padded = with_halo(current, (("circ", 1), ("span", 2)), 1)
        padded = wall_zero(padded, 1)
        return advance(padded, current, q_old, pseudo_rate, inlet_plane, flux_jacobians)

    first_pass = sweep(q_old)
    return sweep(first_pass)


def solution(mesh):
    return jax.shard_map(
        body,
        mesh=mesh,
        in_specs=(
            P(None, "circ", "span", None),
            P("circ", "span", None),
            P(),
            P(None, "circ", "span"),
            P("span"),
            P("circ", "span", None),
            P("circ", "span", None),
            P("circ", "span", None),
            P(),
        ),
        out_specs=P(None, "circ", "span", None),
        check_vma=False,
    )
```

profile of v0, /device:TPU:6, one launch (start us, length us, event | category | flops | bytes accessed | tf_op | source)
XLA Modules:
  0.0 389.9 jit_solution(16798565273600464727)
XLA Ops:
  6.5 1.1 fusion.53
  8.7 1.6 collective-permute-start
  12.1 37.0 %all_gather.3 = f32[5,32,128]{2,0,1:T(8,128)S(1)} all-gather(f32[5,4,128]{2,0,1:T(8,128)S(1)} %copy.72), channel_id=1, replica_groups=mesh['circ'=8,'span'=32] {'circ'}, dimensions={1}, use_global_device_ids=true | all-gather | bytes 92160 | tf_op jit(solution)/shard_map/all_gather | solution.py:70
  49.8 5.9 %gather_fusion = f32[512,5]{1,0:T(8,128)} fusion(f32[5,32,128]{0,2,1:T(8,128)S(1)} %copy.73, s32[512]{0:T(512)S(1)} %fusion.43), kind=kCustom, calls=%fused_computation | custom fusion | bytes 24576 | tf_op jit(solution)/shard_map/jit(take_along_axis)/gather | solution.py:73
  55.7 1.1 copy.87
  57.1 2.3 fusion.34
  59.5 1.5 fusion.54
  61.0 3.4 copy.106
  64.4 2.1 copy.105
  67.9 264.7 %all-reduce.5.cloned.1.call-done = f32[128,5,4,32]{3,0,2,1:T(8,128)} async-done(((f32[128,5,4,32]{3,0,2,1:T(8,128)}), f32[128,5,4,32]{3,0,2,1:T(8,128)}) %all-reduce.5.cloned.1.call-update) | async-done | bytes 327696
  334.3 1.1 constant_dynamic-update-slice_fusion.1
  336.2 1.5 constant_dynamic-update-slice_fusion
  338.0 5.8 %collective-permute-start.3 = (f32[5,6,1,128]{3,0,2,1:T(8,128)S(1)}, f32[5,6,1,128]{3,0,2,1:T(8,128)S(1)}, u32[]{:S(2)}, u32[]{:S(2)}) collective-permute-start(f32[5,6,1,128]{3,0,2,1:T(8,128)S(1)} %get-tuple-element.8), channel_id=1, source_target_pairs={{1,0},{2,1},{3,2},{4,3},{5,4},{6,5},{7,6},{8,7},{9,8},{10,9},{11,1... | collective-permute-start | bytes 46088 | tf_op jit(solution)/shard_map/ppermute | solution.py:24
  343.8 2.5 fusion.18
  346.6 2.0 fusion.20
  348.7 4.9 %fusion.7 = f32[5,4,128,128]{3,0,2,1:T(8,128)S(1)} fusion(f32[4,128,128,5]{2,3,1,0:T(8,128)S(1)} %fusion.18, f32[4,128,128,5]{2,3,1,0:T(8,128)S(1)} %fusion.20, f32[5,6,130,128]{3,0,2,1:T(8,128)S(1)} %maximum_multiply_fusion, f32[5,4,128,127]{3,0,2,1:T(8,128)S(1)} %copy-done.2, f32[4,128,128]{2,1,0:T(8,128)S(1)} %copy-done.3, ...), kind=kOutput, calls=%fused_computation.14 | convolution fusion | flops 25559040 | bytes 25954816 | tf_op jit(solution)/shard_map/fg,gtsa->ftsa/dot_general | solution.py:30
  354.3 1.5 collective-permute-start.5
  356.5 6.5 %collective-permute-done.4 = f32[5,1,128,128]{3,0,2,1:T(8,128)S(1)} collective-permute-done((f32[5,1,128,128]{3,0,2,1:T(8,128)S(1)}, f32[5,1,128,128]{3,0,2,1:T(8,128)S(1)}, u32[]{:S(2)}, u32[]{:S(2)}) %collective-permute-start.4) | collective-permute-done | bytes 327712 | tf_op jit(solution)/shard_map/ppermute | solution.py:21
  362.9 2.7 collective-permute-done.5
  365.7 6.1 %collective-permute-start.7 = (f32[5,6,1,128]{3,0,2,1:T(8,128)S(1)}, f32[5,6,1,128]{3,0,2,1:T(8,128)S(1)}, u32[]{:S(2)}, u32[]{:S(2)}) collective-permute-start(f32[5,6,1,128]{3,0,2,1:T(8,128)S(1)} %get-tuple-element.6), channel_id=1, source_target_pairs={{1,0},{2,1},{3,2},{4,3},{5,4},{6,5},{7,6},{8,7},{9,8},{10,9},{11,1... | collective-permute-start | bytes 46088 | tf_op jit(solution)/shard_map/ppermute | solution.py:24
  371.8 2.5 fusion.8
  374.7 2.0 fusion.10
  376.7 5.0 %fusion.3 = f32[5,4,128,128]{3,0,2,1:T(8,128)S(1)} fusion(f32[5,4,128,128]{3,0,2,1:T(8,128)S(1)} %fusion.7, f32[4,128,128,5]{2,3,1,0:T(8,128)S(1)} %fusion.8, f32[4,128,128,5]{2,3,1,0:T(8,128)S(1)} %fusion.10, f32[5,6,130,128]{3,0,2,1:T(8,128)S(1)} %maximum_multiply_fusion.1, f32[5,4,128,127]{3,0,2,1:T(8,128)S(1)} %get-tuple-element.12, ...), kind=kOutput, calls=%fused_computation.9 | convolution fusion | flops 25559040 | bytes 28051968 | tf_op jit(solution)/shard_map/fg,gtsa->ftsa/dot_general | solution.py:30
  381.7 1.3 copy.82
  (60 shorter events, 9.4 us)
Async XLA Ops:
  6.5 5.3 %copy-start.9 = (s32[128]{0:T(128)S(1)}, s32[128]{0:T(128)}, u32[]{:S(2)}) copy-start(s32[128]{0:T(128)} %param.13) | copy-start | bytes 1540
  6.5 5.6 %copy-start.4 = (f32[5,4,128]{2,1,0:T(4,128)S(1)}, f32[5,4,128]{2,1,0:T(4,128)}, u32[]{:S(2)}) copy-start(f32[5,4,128]{2,1,0:T(4,128)} %param.12) | copy-start | bytes 30724
  6.5 326.1 %all-reduce.5.cloned.1.call-start = ((), (), s32[]{:S(2)}) async-start(), calls=%async_computation | async-start | bytes 2621440
  8.7 48.1 %copy-start.6 = (s32[1,4,4]{2,1,0:T(4,128)S(1)}, s32[1,4,4]{2,1,0:T(4,128)}, u32[]{:S(2)}) copy-start(s32[1,4,4]{2,1,0:T(4,128)} %param.15) | copy-start | bytes 196
  8.7 48.1 %copy-start.7 = (s32[1,4,4]{2,1,0:T(4,128)S(1)}, s32[1,4,4]{2,1,0:T(4,128)}, u32[]{:S(2)}) copy-start(s32[1,4,4]{2,1,0:T(4,128)} %param.14) | copy-start | bytes 196
  8.7 48.2 %copy-start.8 = (s32[1,4,4]{2,1,0:T(4,128)S(1)}, s32[1,4,4]{2,1,0:T(4,128)}, u32[]{:S(2)}) copy-start(s32[1,4,4]{2,1,0:T(4,128)} %param.16) | copy-start | bytes 196
  8.7 48.2 %copy-start.10 = (f32[16]{0:T(128)S(1)}, f32[16]{0:T(128)}, u32[]{:S(2)}) copy-start(f32[16]{0:T(128)} %param.17) | copy-start | bytes 196
  8.7 325.6 %collective-permute-start = (f32[5,1,128,128]{3,0,2,1:T(8,128)}, f32[5,1,128,128]{3,0,2,1:T(8,128)}, u32[]{:S(2)}, u32[]{:S(2)}) collective-permute-start(f32[5,1,128,128]{3,0,2,1:T(8,128)} %copy.107), channel_id=1, source_target_pairs={{0,32},{32,64},{64,96},{96,128},{128,160},{160,192},{192,224},{224... | collective-permute-start | bytes 983048 | tf_op jit(solution)/shard_map/ppermute | solution.py:21
  11.3 324.9 %collective-permute-start.1 = (f32[5,1,128,128]{3,0,2,1:T(8,128)}, f32[5,1,128,128]{3,0,2,1:T(8,128)}, u32[]{:S(2)}, u32[]{:S(2)}) collective-permute-start(f32[5,1,128,128]{3,0,2,1:T(8,128)} %copy.108), channel_id=1, source_target_pairs={{32,0},{64,32},{96,64},{128,96},{160,128},{192,160},{224,192},{0,2... | collective-permute-start | bytes 983048 | tf_op jit(solution)/shard_map/ppermute | solution.py:24
  49.8 9.7 %copy-start = (f32[5,4,128,128]{3,2,1,0:T(8,128)S(1)}, f32[5,4,128,128]{3,2,1,0:T(8,128)}, u32[]{:S(2)}) copy-start(f32[5,4,128,128]{3,2,1,0:T(8,128)} %param.9) | copy-start | bytes 3932164
  64.4 2.2 copy-start.11
  64.4 3.4 copy-start.5
  335.4 8.4 %copy-start.1 = (f32[5,4,128,127]{3,0,2,1:T(8,128)S(1)}, f32[5,4,128,127]{3,0,2,1:T(8,128)}, u32[]{:S(2)}) copy-start(f32[5,4,128,127]{3,0,2,1:T(8,128)} %copy.106) | copy-start | bytes 3901444
  335.4 8.4 %copy-start.2 = (f32[5,4,128,127]{3,0,2,1:T(8,128)S(1)}, f32[5,4,128,127]{3,0,2,1:T(8,128)}, u32[]{:S(2)}) copy-start(f32[5,4,128,127]{3,0,2,1:T(8,128)} %copy.105) | copy-start | bytes 3901444
  337.8 8.5 %collective-permute-start.2 = (f32[5,6,1,128]{3,0,2,1:T(8,128)S(1)}, f32[5,6,1,128]{3,0,2,1:T(8,128)S(1)}, u32[]{:S(2)}, u32[]{:S(2)}) collective-permute-start(f32[5,6,1,128]{3,0,2,1:T(8,128)S(1)} %get-tuple-element.7), channel_id=1, source_target_pairs={{0,1},{1,2},{2,3},{3,4},{4,5},{5,6},{6,7},{7,8},{8,9},{9,10},{10,1... | collective-permute-start | bytes 46088 | tf_op jit(solution)/shard_map/ppermute | solution.py:21
  338.0 8.3 %collective-permute-start.3 = (f32[5,6,1,128]{3,0,2,1:T(8,128)S(1)}, f32[5,6,1,128]{3,0,2,1:T(8,128)S(1)}, u32[]{:S(2)}, u32[]{:S(2)}) collective-permute-start(f32[5,6,1,128]{3,0,2,1:T(8,128)S(1)} %get-tuple-element.8), channel_id=1, source_target_pairs={{1,0},{2,1},{3,2},{4,3},{5,4},{6,5},{7,6},{8,7},{9,8},{10,9},{11,1... | collective-permute-start | bytes 46088 | tf_op jit(solution)/shard_map/ppermute | solution.py:24
  346.6 2.0 copy-start.3
  353.7 9.3 %collective-permute-start.4 = (f32[5,1,128,128]{3,0,2,1:T(8,128)S(1)}, f32[5,1,128,128]{3,0,2,1:T(8,128)S(1)}, u32[]{:S(2)}, u32[]{:S(2)}) collective-permute-start(f32[5,1,128,128]{3,0,2,1:T(8,128)S(1)} %get-tuple-element.9), channel_id=1, source_target_pairs={{0,32},{32,64},{64,96},{96,128},{128,160},{160,192},{192,224},{224... | collective-permute-start | bytes 983048 | tf_op jit(solution)/shard_map/ppermute | solution.py:21
  354.3 11.3 %collective-permute-start.5 = (f32[5,1,128,128]{3,0,2,1:T(8,128)S(1)}, f32[5,1,128,128]{3,0,2,1:T(8,128)S(1)}, u32[]{:S(2)}, u32[]{:S(2)}) collective-permute-start(f32[5,1,128,128]{3,0,2,1:T(8,128)S(1)} %get-tuple-element.10), channel_id=1, source_target_pairs={{32,0},{64,32},{96,64},{128,96},{160,128},{192,160},{224,192},{0,2... | collective-permute-start | bytes 983048 | tf_op jit(solution)/shard_map/ppermute | solution.py:24
  365.6 8.7 %collective-permute-start.6 = (f32[5,6,1,128]{3,0,2,1:T(8,128)S(1)}, f32[5,6,1,128]{3,0,2,1:T(8,128)S(1)}, u32[]{:S(2)}, u32[]{:S(2)}) collective-permute-start(f32[5,6,1,128]{3,0,2,1:T(8,128)S(1)} %get-tuple-element.5), channel_id=1, source_target_pairs={{0,1},{1,2},{2,3},{3,4},{4,5},{5,6},{6,7},{7,8},{8,9},{9,10},{10,1... | collective-permute-start | bytes 46088 | tf_op jit(solution)/shard_map/ppermute | solution.py:21
  365.7 8.6 %collective-permute-start.7 = (f32[5,6,1,128]{3,0,2,1:T(8,128)S(1)}, f32[5,6,1,128]{3,0,2,1:T(8,128)S(1)}, u32[]{:S(2)}, u32[]{:S(2)}) collective-permute-start(f32[5,6,1,128]{3,0,2,1:T(8,128)S(1)} %get-tuple-element.6), channel_id=1, source_target_pairs={{1,0},{2,1},{3,2},{4,3},{5,4},{6,5},{7,6},{8,7},{9,8},{10,9},{11,1... | collective-permute-start | bytes 46088 | tf_op jit(solution)/shard_map/ppermute | solution.py:24
Sparse Core Ops, SparseCore 0:
  59.6 272.9 all-reduce.4
where the time goes:
time: 390 us
  waiting for transfers between devices  274 us (70%)
  blocking collectives  37 us (9%)
  local copies, waits for them, and re-layouts  25.8 us (7%)
  matrix products  21.3 us (5%)
  starting transfers between devices  16.4 us (4%)
  between operations  14.4 us (4%)
    unnamed x2, waiting for transfers between devices  265 us
    all_gather x1, blocking collectives, body(): all_rows = lax.all_gather(rotor_face, 'circ', axis=1, tiled=True)  37 us
    dot_general x6, matrix products, contract(): jnp.einsum('fg,gtsa->ftsa', matrix, values, precision=lax.Precision.HIGHEST)  18.9 us
    ppermute x4, starting transfers between devices, with_halo(): lax.ppermute(lax.slice_in_dim(block, 0, width, axis=dim), axis, backward)  13.8 us
    unnamed x32, local copies, waits for them, and re-layouts  10.2 us
  transfers between devices with their start and end apart: 9, of which 3 were waited for; matrix products, arithmetic and copies ran while one was open for 7% of the time, Pallas kernels for 0%

commit v1 on v0

--- a/solution.py
+++ b/solution.py
@@ -80,12 +80,11 @@
     mixing = jnp.sum(
         jnp.where(targets[None] == panel_ids[:, None, None], local_weights[None], 0.0), axis=-1
     )
-    own_panels = lax.psum_scatter(
-        jnp.einsum("gk,ftkp->gftp", mixing, panels, precision=lax.Precision.HIGHEST),
-        "span",
-        scatter_dimension=0,
-        tiled=True,
-    )
+    span_count = lax.axis_size("span")
+    contributions = jnp.einsum("gk,ftkp->gftp", mixing, panels, precision=lax.Precision.HIGHEST)
+    contributions = contributions.reshape((span_count, KP_DEV) + contributions.shape[1:])
+    received = lax.all_to_all(contributions, "span", 0, 0, tiled=True)
+    own_panels = jnp.sum(received, axis=0)
     inlet_plane = jnp.transpose(own_panels, (1, 2, 0, 3)).reshape(NF, rows_local, KP_DEV * PW)
 
     def sweep(current):

time: 390 us -> 128 us (0.33)
  waiting for transfers between devices: 274 us -> 10.4 us
  between operations: 14.4 us -> 0.44 us
  starting transfers between devices: 16.4 us -> 26.4 us
  matrix products: 21.3 us -> 26.1 us
    unnamed x2 -> x0, waiting for transfers between devices: 265 us -> none
    all_to_all x0 -> x1, starting transfers between devices: none -> 11.2 us  [body(): received = lax.all_to_all(contributions, 'span', 0, 0, tiled=True)]
    dot_general x6, matrix products: 18.9 us -> 24.9 us  [contract(): jnp.einsum('fg,gtsa->ftsa', matrix, values, precision=lax.Precision.HIGHEST)]
    unnamed x32 -> x35, local copies, waits for them, and re-layouts: 10.2 us -> 12.2 us
  transfers between devices with their start and end apart: 9 -> 9, of which waited for: 3 -> 2; matrix products, arithmetic and copies ran while one was open for 7% -> 19% of each run, Pallas kernels for 0% -> 0%
where the time goes in v1:
time: 128 us
  blocking collectives  36.6 us (29%)
  starting transfers between devices  26.4 us (21%)
  matrix products  26.1 us (20%)
  local copies, waits for them, and re-layouts  25.1 us (20%)
  waiting for transfers between devices  10.4 us (8%)
  other arithmetic  3.01 us (2%)
    all_gather x1, blocking collectives, body(): all_rows = lax.all_gather(rotor_face, 'circ', axis=1, tiled=True)  36.6 us
    dot_general x6, matrix products, contract(): jnp.einsum('fg,gtsa->ftsa', matrix, values, precision=lax.Precision.HIGHEST)  24.9 us
    ppermute x4, starting transfers between devices, with_halo(): lax.ppermute(lax.slice_in_dim(block, 0, width, axis=dim), axis, backward)  13.3 us
    unnamed x35, local copies, waits for them, and re-layouts  12.2 us
    all_to_all x1, starting transfers between devices, body(): received = lax.all_to_all(contributions, 'span', 0, 0, tiled=True)  11.2 us
    ppermute x4, waiting for transfers between devices, with_halo(): lax.ppermute(lax.slice_in_dim(block, block.shape[dim] - width, None, axis...  7.96 us
    gather x1, local copies, waits for them, and re-layouts, body(): rotated = jnp.take_along_axis(all_rows, source_rows[None], axis=1)  3.52 us
  transfers between devices with their start and end apart: 9, of which 2 were waited for; matrix products, arithmetic and copies ran while one was open for 19% of the time, Pallas kernels for 0%

profile of v1, /device:TPU:6, one launch (start us, length us, event | category | flops | bytes accessed | tf_op | source)
XLA Modules:
  0.0 128.1 jit_solution(10286612032993077256)
XLA Ops:
  0.0 1.2 fusion.49
  2.2 1.5 %collective-permute-start = (f32[5,1,128,128]{3,0,2,1:T(8,128)}, f32[5,1,128,128]{3,0,2,1:T(8,128)}, u32[]{:S(2)}, u32[]{:S(2)}) collective-permute-start(f32[5,1,128,128]{3,0,2,1:T(8,128)} %copy.118), channel_id=1, source_target_pairs={{0,32},{32,64},{64,96},{96,128},{128,160},{160,192},{192,224},{224... | collective-permute-start | bytes 983048 | tf_op jit(solution)/shard_map/ppermute | solution.py:21
  6.0 36.6 %all_gather.3 = f32[5,32,128]{2,0,1:T(8,128)S(1)} all-gather(f32[5,4,128]{2,0,1:T(8,128)S(1)} %copy.76), channel_id=1, replica_groups=mesh['circ'=8,'span'=32] {'circ'}, dimensions={1}, use_global_device_ids=true | all-gather | bytes 92160 | tf_op jit(solution)/shard_map/all_gather | solution.py:70
  43.2 3.5 %gather_fusion = f32[512,5]{1,0:T(8,128)S(1)} fusion(f32[5,32,128]{0,2,1:T(8,128)S(1)} %copy.77, s32[512]{0:T(512)S(1)} %fusion.41), kind=kCustom, calls=%fused_computation | custom fusion | bytes 24576 | tf_op jit(solution)/shard_map/jit(take_along_axis)/gather | solution.py:73
  47.0 1.3 fusion.34
  49.2 1.6 %reshape.183 = f32[32,1,2560]{2,1,0:T(1,128)} reshape(f32[32,4,5,4,32]{4,3,2,1,0:T(4,128)S(1)} %copy.80) | data formatting | bytes 655360
  50.7 11.2 %all-to-all-start = ((f32[32,1,2560]{2,1,0:T(1,128)}), f32[32,1,2560]{2,1,0:T(1,128)S(1)}, u32[]{:S(2)}, u32[]{:S(2)}) async-start(f32[32,1,2560]{2,1,0:T(1,128)} %reshape.183), calls=%async_computation | async-start | bytes 655360 | tf_op jit(solution)/shard_map/all_to_all | solution.py:86
  65.8 5.2 %collective-permute-start.3 = (f32[5,6,1,128]{3,0,2,1:T(8,128)S(1)}, f32[5,6,1,128]{3,0,2,1:T(8,128)S(1)}, u32[]{:S(2)}, u32[]{:S(2)}) collective-permute-start(f32[5,6,1,128]{3,0,2,1:T(8,128)S(1)} %get-tuple-element.8), channel_id=1, source_target_pairs={{1,0},{2,1},{3,2},{4,3},{5,4},{6,5},{7,6},{8,7},{9,8},{10,9},{11,1... | collective-permute-start | bytes 46088 | tf_op jit(solution)/shard_map/ppermute | solution.py:24
  71.0 2.2 %copy.117 = f32[5,4,128,127]{3,0,2,1:T(8,128)} copy(f32[5,4,128,127]{3,2,1,0:T(8,128)S(1)} %get-tuple-element.15) | data formatting | bytes 2600960
  73.2 2.2 %copy.116 = f32[5,4,128,127]{3,0,2,1:T(8,128)} copy(f32[5,4,128,127]{3,2,1,0:T(8,128)S(1)} %get-tuple-element.16) | data formatting | bytes 2600960
  75.7 1.7 %copy-done.3 = f32[5,6,130,128]{3,0,2,1:T(8,128)} copy-done((f32[5,6,130,128]{3,0,2,1:T(8,128)}, f32[5,6,130,128]{3,0,2,1:T(8,128)S(1)}, u32[]{:S(2)}) %copy-start.3) | copy-done | bytes 1996824
  77.4 3.4 %fusion.20 = f32[4,128,128,5]{2,3,1,0:T(8,128)} fusion(f32[5,6,130,128]{3,0,2,1:T(8,128)S(1)} %maximum_multiply_fusion, f32[1,5,5]{2,0,1:T(1,128)S(1)} %get-tuple-element.18), kind=kOutput, calls=%fused_computation.25 | convolution fusion | flops 19988480 | bytes 5507584 | tf_op jit(solution)/shard_map/fg,gtsa->ftsa/dot_general | solution.py:30
  81.3 1.4 %reduce.1 = f32[32,2560]{1,0:T(8,128)S(1)} reduce(f32[32,1,2560]{2,1,0:T(1,128)S(1)} %all-to-all-done, f32[]{:T(128)} %broadcast.283), dimensions={1}, to_apply=%all_to_all.3.reduce_sub_computation | reduce | bytes 655364 | tf_op jit(solution)/shard_map/all_to_all | solution.py:86
  84.5 1.4 %reshape.182 = f32[5,4,128,1]{3,0,2,1:T(8,128)S(1)} reshape(f32[5,4,4,32]{0,3,2,1:T(8,128)} %copy.98) | data formatting | bytes 20480 | tf_op jit(solution)/shard_map/broadcast_in_dim;reshape | solution.py:40
  86.0 4.9 %fusion.18 = f32[4,128,128,5]{2,3,1,0:T(8,128)S(1)} fusion(f32[5,4,128,127]{3,0,2,1:T(8,128)} %copy.116, f32[5,4,128,127]{3,0,2,1:T(8,128)} %copy.117, f32[5,4,128,1]{3,0,2,1:T(8,128)S(1)} %reshape.182, f32[1,5,5]{2,0,1:T(1,128)S(1)} %get-tuple-element.19), kind=kOutput, calls=%fused_computation.23 | convolution fusion | flops 20316160 | bytes 3922020 | tf_op jit(solution)/shard_map/fg,gtsa->ftsa/dot_general | solution.py:30
  90.9 7.1 %fusion.7 = f32[5,4,128,128]{3,0,2,1:T(8,128)S(1)} fusion(f32[4,128,128,5]{2,3,1,0:T(8,128)S(1)} %fusion.18, f32[4,128,128,5]{2,3,1,0:T(8,128)} %fusion.20, f32[5,6,130,128]{3,0,2,1:T(8,128)S(1)} %copy-done.4, f32[5,4,128,127]{3,0,2,1:T(8,128)S(1)} %copy-done.2, f32[4,128,128]{2,1,0:T(8,128)S(1)} %copy-done.5, f32[5,4,128,128]{3,2,1,0:T(8,128)S(1)} %copy-done, ...), kind=kOutput, calls=%fused_computation.14 | convolution fusion | flops 25559040 | bytes 25168384 | tf_op jit(solution)/shard_map/fg,gtsa->ftsa/dot_general | solution.py:30
  98.2 2.0 %collective-permute-start.5 = (f32[5,1,128,128]{3,0,2,1:T(8,128)S(1)}, f32[5,1,128,128]{3,0,2,1:T(8,128)S(1)}, u32[]{:S(2)}, u32[]{:S(2)}) collective-permute-start(f32[5,1,128,128]{3,0,2,1:T(8,128)S(1)} %get-tuple-element.10), channel_id=1, source_target_pairs={{32,0},{64,32},{96,64},{128,96},{160,128},{192,160},{224,192},{0,2... | collective-permute-start | bytes 983048 | tf_op jit(solution)/shard_map/ppermute | solution.py:24
  100.9 7.9 %collective-permute-done.4 = f32[5,1,128,128]{3,0,2,1:T(8,128)S(1)} collective-permute-done((f32[5,1,128,128]{3,0,2,1:T(8,128)S(1)}, f32[5,1,128,128]{3,0,2,1:T(8,128)S(1)}, u32[]{:S(2)}, u32[]{:S(2)}) %collective-permute-start.4) | collective-permute-done | bytes 327712 | tf_op jit(solution)/shard_map/ppermute | solution.py:21
  108.8 2.4 %collective-permute-done.5 = f32[5,1,128,128]{3,0,2,1:T(8,128)S(1)} collective-permute-done((f32[5,1,128,128]{3,0,2,1:T(8,128)S(1)}, f32[5,1,128,128]{3,0,2,1:T(8,128)S(1)}, u32[]{:S(2)}, u32[]{:S(2)}) %collective-permute-start.5) | collective-permute-done | bytes 327712 | tf_op jit(solution)/shard_map/ppermute | solution.py:24
  111.3 5.5 %collective-permute-start.7 = (f32[5,6,1,128]{3,0,2,1:T(8,128)S(1)}, f32[5,6,1,128]{3,0,2,1:T(8,128)S(1)}, u32[]{:S(2)}, u32[]{:S(2)}) collective-permute-start(f32[5,6,1,128]{3,0,2,1:T(8,128)S(1)} %get-tuple-element.6), channel_id=1, source_target_pairs={{1,0},{2,1},{3,2},{4,3},{5,4},{6,5},{7,6},{8,7},{9,8},{10,9},{11,1... | collective-permute-start | bytes 46088 | tf_op jit(solution)/shard_map/ppermute | solution.py:24
  116.8 2.5 %fusion.8 = f32[4,128,128,5]{2,3,1,0:T(8,128)S(1)} fusion(f32[5,4,128,127]{3,0,2,1:T(8,128)S(1)} %get-tuple-element.12, f32[5,4,128,127]{3,0,2,1:T(8,128)S(1)} %get-tuple-element.11, f32[5,4,128,1]{3,0,2,1:T(8,128)S(1)} %reshape.182, f32[1,5,5]{2,0,1:T(1,128)S(1)} %get-tuple-element.19), kind=kOutput, calls=%fused_computation.15 | convolution fusion | flops 20316160 | bytes 3922020 | tf_op jit(solution)/shard_map/fg,gtsa->ftsa/dot_general | solution.py:30
  119.7 2.0 %fusion.10 = f32[4,128,128,5]{2,3,1,0:T(8,128)S(1)} fusion(f32[5,6,130,128]{3,0,2,1:T(8,128)S(1)} %maximum_multiply_fusion.1, f32[1,5,5]{2,0,1:T(1,128)S(1)} %get-tuple-element.18), kind=kOutput, calls=%fused_computation.17 | convolution fusion | flops 19988480 | bytes 5507584 | tf_op jit(solution)/shard_map/fg,gtsa->ftsa/dot_general | solution.py:30
  121.7 5.0 %fusion.3 = f32[5,4,128,128]{3,0,2,1:T(8,128)S(1)} fusion(f32[5,4,128,128]{3,0,2,1:T(8,128)S(1)} %fusion.7, f32[4,128,128,5]{2,3,1,0:T(8,128)S(1)} %fusion.8, f32[4,128,128,5]{2,3,1,0:T(8,128)S(1)} %fusion.10, f32[5,6,130,128]{3,0,2,1:T(8,128)S(1)} %maximum_multiply_fusion.1, f32[5,4,128,127]{3,0,2,1:T(8,128)S(1)} %get-tuple-element.12, ...), kind=kOutput, calls=%fused_computation.9 | convolution fusion | flops 25559040 | bytes 28051968 | tf_op jit(solution)/shard_map/fg,gtsa->ftsa/dot_general | solution.py:30
  126.8 1.3 %copy.90 = f32[5,4,128,128]{3,2,1,0:T(8,128)} copy(f32[5,4,128,128]{3,0,2,1:T(8,128)S(1)} %fusion.3) | data formatting | bytes 2621440 | tf_op jit(solution)/shard_map/sub | solution.py:48
  (67 shorter events, 12.8 us)
Async XLA Ops:
  0.0 5.3 %copy-start.12 = (s32[128]{0:T(128)S(1)}, s32[128]{0:T(128)}, u32[]{:S(2)}) copy-start(s32[128]{0:T(128)} %param.13) | copy-start | bytes 1540
  0.0 5.4 %copy-start.6 = (f32[5,4,128]{2,1,0:T(4,128)S(1)}, f32[5,4,128]{2,1,0:T(4,128)}, u32[]{:S(2)}) copy-start(f32[5,4,128]{2,1,0:T(4,128)} %param.12) | copy-start | bytes 30724
  0.0 5.4 %copy-start.8 = (s32[1,4,4]{2,1,0:T(4,128)S(1)}, s32[1,4,4]{2,1,0:T(4,128)}, u32[]{:S(2)}) copy-start(s32[1,4,4]{2,1,0:T(4,128)} %param.15) | copy-start | bytes 196
  0.0 5.4 %copy-start.9 = (s32[1,4,4]{2,1,0:T(4,128)S(1)}, s32[1,4,4]{2,1,0:T(4,128)}, u32[]{:S(2)}) copy-start(s32[1,4,4]{2,1,0:T(4,128)} %param.14) | copy-start | bytes 196
  0.0 5.5 %copy-start.11 = (f32[16]{0:T(128)S(1)}, f32[16]{0:T(128)}, u32[]{:S(2)}) copy-start(f32[16]{0:T(128)} %param.17) | copy-start | bytes 196
  0.0 5.5 %copy-start.10 = (s32[1,4,4]{2,1,0:T(4,128)S(1)}, s32[1,4,4]{2,1,0:T(4,128)}, u32[]{:S(2)}) copy-start(s32[1,4,4]{2,1,0:T(4,128)} %param.16) | copy-start | bytes 196
  2.2 60.2 %collective-permute-start = (f32[5,1,128,128]{3,0,2,1:T(8,128)}, f32[5,1,128,128]{3,0,2,1:T(8,128)}, u32[]{:S(2)}, u32[]{:S(2)}) collective-permute-start(f32[5,1,128,128]{3,0,2,1:T(8,128)} %copy.118), channel_id=1, source_target_pairs={{0,32},{32,64},{64,96},{96,128},{128,160},{160,192},{192,224},{224... | collective-permute-start | bytes 983048 | tf_op jit(solution)/shard_map/ppermute | solution.py:21
  4.7 59.6 %collective-permute-start.1 = (f32[5,1,128,128]{3,0,2,1:T(8,128)}, f32[5,1,128,128]{3,0,2,1:T(8,128)}, u32[]{:S(2)}, u32[]{:S(2)}) collective-permute-start(f32[5,1,128,128]{3,0,2,1:T(8,128)} %copy.119), channel_id=1, source_target_pairs={{32,0},{64,32},{96,64},{128,96},{160,128},{192,160},{224,192},{0,2... | collective-permute-start | bytes 983048 | tf_op jit(solution)/shard_map/ppermute | solution.py:24
  48.3 13.7 %copy-start.7 = (f32[3,5,5]{2,0,1:T(4,128)S(1)}, f32[3,5,5]{2,0,1:T(4,128)}, u32[]{:S(2)}) copy-start(f32[3,5,5]{2,0,1:T(4,128)} %param.11) | copy-start | bytes 904
  48.3 13.7 %copy-start = (f32[5,4,128,128]{3,2,1,0:T(8,128)S(1)}, f32[5,4,128,128]{3,2,1,0:T(8,128)}, u32[]{:S(2)}) copy-start(f32[5,4,128,128]{3,2,1,0:T(8,128)} %param.9) | copy-start | bytes 3932164
  50.7 30.0 %all-to-all-start = ((f32[32,1,2560]{2,1,0:T(1,128)}), f32[32,1,2560]{2,1,0:T(1,128)S(1)}, u32[]{:S(2)}, u32[]{:S(2)}) async-start(f32[32,1,2560]{2,1,0:T(1,128)} %reshape.183), calls=%async_computation | async-start | bytes 655360 | tf_op jit(solution)/shard_map/all_to_all | solution.py:86
  65.4 9.9 %collective-permute-start.2 = (f32[5,6,1,128]{3,0,2,1:T(8,128)S(1)}, f32[5,6,1,128]{3,0,2,1:T(8,128)S(1)}, u32[]{:S(2)}, u32[]{:S(2)}) collective-permute-start(f32[5,6,1,128]{3,0,2,1:T(8,128)S(1)} %get-tuple-element.7), channel_id=1, source_target_pairs={{0,1},{1,2},{2,3},{3,4},{4,5},{5,6},{6,7},{7,8},{8,9},{9,10},{10,1... | collective-permute-start | bytes 46088 | tf_op jit(solution)/shard_map/ppermute | solution.py:21
  65.8 9.6 %collective-permute-start.3 = (f32[5,6,1,128]{3,0,2,1:T(8,128)S(1)}, f32[5,6,1,128]{3,0,2,1:T(8,128)S(1)}, u32[]{:S(2)}, u32[]{:S(2)}) collective-permute-start(f32[5,6,1,128]{3,0,2,1:T(8,128)S(1)} %get-tuple-element.8), channel_id=1, source_target_pairs={{1,0},{2,1},{3,2},{4,3},{5,4},{6,5},{7,6},{8,7},{9,8},{10,9},{11,1... | collective-permute-start | bytes 46088 | tf_op jit(solution)/shard_map/ppermute | solution.py:24
  75.7 1.7 %copy-start.3 = (f32[5,6,130,128]{3,0,2,1:T(8,128)}, f32[5,6,130,128]{3,0,2,1:T(8,128)S(1)}, u32[]{:S(2)}) copy-start(f32[5,6,130,128]{3,0,2,1:T(8,128)S(1)} %maximum_multiply_fusion) | copy-start | bytes 5990404
  85.9 4.9 %copy-start.1 = (f32[5,4,128,127]{3,0,2,1:T(8,128)S(1)}, f32[5,4,128,127]{3,0,2,1:T(8,128)}, u32[]{:S(2)}) copy-start(f32[5,4,128,127]{3,0,2,1:T(8,128)} %copy.117) | copy-start | bytes 3901444
  86.0 4.9 %copy-start.2 = (f32[5,4,128,127]{3,0,2,1:T(8,128)S(1)}, f32[5,4,128,127]{3,0,2,1:T(8,128)}, u32[]{:S(2)}) copy-start(f32[5,4,128,127]{3,0,2,1:T(8,128)} %copy.116) | copy-start | bytes 3901444
  86.0 4.9 %copy-start.4 = (f32[5,6,130,128]{3,0,2,1:T(8,128)S(1)}, f32[5,6,130,128]{3,0,2,1:T(8,128)}, u32[]{:S(2)}) copy-start(f32[5,6,130,128]{3,0,2,1:T(8,128)} %copy-done.3) | copy-start | bytes 5990404
  86.0 4.9 %copy-start.5 = (f32[4,128,128]{2,1,0:T(8,128)S(1)}, f32[4,128,128]{2,1,0:T(8,128)}, u32[]{:S(2)}) copy-start(f32[4,128,128]{2,1,0:T(8,128)} %param.10) | copy-start | bytes 786436
  98.1 10.7 %collective-permute-start.4 = (f32[5,1,128,128]{3,0,2,1:T(8,128)S(1)}, f32[5,1,128,128]{3,0,2,1:T(8,128)S(1)}, u32[]{:S(2)}, u32[]{:S(2)}) collective-permute-start(f32[5,1,128,128]{3,0,2,1:T(8,128)S(1)} %get-tuple-element.9), channel_id=1, source_target_pairs={{0,32},{32,64},{64,96},{96,128},{128,160},{160,192},{192,224},{224... | collective-permute-start | bytes 983048 | tf_op jit(solution)/shard_map/ppermute | solution.py:21
  98.2 13.1 %collective-permute-start.5 = (f32[5,1,128,128]{3,0,2,1:T(8,128)S(1)}, f32[5,1,128,128]{3,0,2,1:T(8,128)S(1)}, u32[]{:S(2)}, u32[]{:S(2)}) collective-permute-start(f32[5,1,128,128]{3,0,2,1:T(8,128)S(1)} %get-tuple-element.10), channel_id=1, source_target_pairs={{32,0},{64,32},{96,64},{128,96},{160,128},{192,160},{224,192},{0,2... | collective-permute-start | bytes 983048 | tf_op jit(solution)/shard_map/ppermute | solution.py:24
  111.2 8.1 %collective-permute-start.6 = (f32[5,6,1,128]{3,0,2,1:T(8,128)S(1)}, f32[5,6,1,128]{3,0,2,1:T(8,128)S(1)}, u32[]{:S(2)}, u32[]{:S(2)}) collective-permute-start(f32[5,6,1,128]{3,0,2,1:T(8,128)S(1)} %get-tuple-element.5), channel_id=1, source_target_pairs={{0,1},{1,2},{2,3},{3,4},{4,5},{5,6},{6,7},{7,8},{8,9},{9,10},{10,1... | collective-permute-start | bytes 46088 | tf_op jit(solution)/shard_map/ppermute | solution.py:21
  111.3 8.0 %collective-permute-start.7 = (f32[5,6,1,128]{3,0,2,1:T(8,128)S(1)}, f32[5,6,1,128]{3,0,2,1:T(8,128)S(1)}, u32[]{:S(2)}, u32[]{:S(2)}) collective-permute-start(f32[5,6,1,128]{3,0,2,1:T(8,128)S(1)} %get-tuple-element.6), channel_id=1, source_target_pairs={{1,0},{2,1},{3,2},{4,3},{5,4},{6,5},{7,6},{8,7},{9,8},{10,9},{11,1... | collective-permute-start | bytes 46088 | tf_op jit(solution)/shard_map/ppermute | solution.py:24
